TPU v7x, 32 devices: a whole 2x2x4 slice. The times are simulated.
32 devices in a mesh: seq: 8 (over z, y), fsdp: 4 (over x, core).
Axes of the slice: x: 2, y: 2, z: 4, core: 2. Of those that a mesh axis runs over, the one named last changes fastest.
Arguments:
- inputs: bfloat16 [12288, 1536], P(('seq', 'fsdp')), may hold values from -15 to 15
- layer_norm_gain: float32 [1536], replicated, may hold values from 0.25 to 1.75
- layer_norm_bias: float32 [1536], replicated, may hold values from -4 to 4
- w_in: bfloat16 [1536, 3072], P('fsdp'), may hold values from -0.15625 to 0.15625
- dw_kernel: float32 [32, 1536], replicated, may hold values from -1 to 1
- bn_gain: float32 [1536], replicated, may hold values from 0.25 to 1.75
- bn_bias: float32 [1536], replicated, may hold values from -4 to 4
- cotangent: bfloat16 [12288, 1536], P(('seq', 'fsdp')), may hold values from -6 to 6
Outputs:
- output: bfloat16 [12288, 1536], P(('seq', 'fsdp'))
- input_gradient: bfloat16 [12288, 1536], P(('seq', 'fsdp'))
- grad_w_in: float32 [1536, 3072], P('fsdp')
- grad_kernel: float32 [32, 1536], replicated
- grad_bn_gain: float32 [1536], replicated
- grad_bn_bias: float32 [1536], replicated
- layer_norm_gain_gradient: float32 [1536], replicated
- grad_ln_bias: float32 [1536], replicated
All inputs are finite; a program needn't handle non-finite values.
Results may differ from a plain program's by a relative error of at most 0.012.
The roundings to bfloat16 on the way count: a program that leaves them out, or rounds other values in their place, can miss the bound.
Values may be sent and summed in bfloat16 or wider, within the bound.
No kernel may reach another device: no remote copies, remote signals or barrier semaphores. Data moves between devices by JAX's collectives and lax.ppermute only.
A program may use at most 128 MiB of HBM per device.

v0:
```python
import jax
import jax.numpy as jnp
from jax import lax
from jax.sharding import PartitionSpec as P

epsilon = 1e-05


def from_behind(block, axis, distance):
    devices = range(lax.axis_size(axis))
    route = [(i - distance, i) for i in devices if i - distance in devices]
    return lax.ppermute(block, axis, route)


def tree_sum(tree, axis):
    count = lax.axis_size(axis)
    if count & count - 1:
        return lax.psum(tree, axis)
    stride = 1
    while stride < count:
        route = [(i, i ^ stride) for i in range(count)]
        tree = jax.tree.map(lambda x: x + lax.ppermute(x, axis, route), tree)
        stride *= 2
    return tree


def on_device(
    inputs, layer_norm_gain, layer_norm_bias, w_in, dw_kernel, bn_gain, bn_bias, cotangent
):
    tok_rows = inputs.shape[0]
    features = inputs.shape[1]
    kernel_len = dw_kernel.shape[0]
    all_frames = tok_rows * lax.axis_size("seq") * lax.axis_size("fsdp")
    frames = inputs.astype(jnp.float32)
    row_mean = jnp.mean(frames, axis=-1, keepdims=True)
    centered_rows = frames - row_mean
    row_inverse_deviation = lax.rsqrt(
        jnp.mean(centered_rows * centered_rows, axis=-1, keepdims=True) + epsilon
    )
    standardized_input = centered_rows * row_inverse_deviation
    normalized_rows = (standardized_input * layer_norm_gain + layer_norm_bias).astype(jnp.bfloat16)
    full_weight = lax.all_gather(w_in, "fsdp", axis=0, tiled=True)
    hidden = jnp.dot(normalized_rows, full_weight, preferred_element_type=jnp.float32)
    value_part = hidden[:, :features]
    gate_sig = jax.nn.sigmoid(hidden[:, features:])
    glu = (value_part * gate_sig).astype(jnp.bfloat16)
    past_rim = from_behind(glu[tok_rows - (kernel_len - 1) :], ("seq", "fsdp"), 1)
    padded_glu = jnp.concatenate([past_rim, glu], axis=0).astype(jnp.float32)
    conv_out = jnp.zeros((tok_rows, features), jnp.float32)
    for offset in range(kernel_len):
        conv_out = (
            conv_out
            + dw_kernel[offset]
            * padded_glu[kernel_len - 1 - offset : kernel_len - 1 - offset + tok_rows]
        )
    chan_mean = tree_sum(jnp.sum(conv_out, axis=0), ("seq", "fsdp")) / all_frames
    conv_centred = conv_out - chan_mean
    chan_var = tree_sum(jnp.sum(conv_centred * conv_centred, axis=0), ("seq", "fsdp")) / all_frames
    bn_rstd = lax.rsqrt(chan_var + epsilon)
    chat = conv_centred * bn_rstd
    z_value = chat * bn_gain + bn_bias
    z_sig = jax.nn.sigmoid(z_value)
    output = (z_value * z_sig).astype(jnp.bfloat16)
    grad_z = cotangent.astype(jnp.float32) * z_sig * (1.0 + z_value * (1.0 - z_sig))
    grad_bn_bias, grad_bn_gain = tree_sum(
        (jnp.sum(grad_z, axis=0), jnp.sum(grad_z * chat, axis=0)), ("seq", "fsdp")
    )
    grad_conv = (
        bn_gain * bn_rstd * (grad_z - grad_bn_bias / all_frames - chat * grad_bn_gain / all_frames)
    )
    future_rim = from_behind(grad_conv[: kernel_len - 1], ("seq", "fsdp"), -1)
    padded_grad = jnp.concatenate([grad_conv, future_rim], axis=0)
    grad_glu = jnp.zeros((tok_rows, features), jnp.float32)
    kernel_rows = []
    for offset in range(kernel_len):
        grad_glu = grad_glu + dw_kernel[offset] * padded_grad[offset : offset + tok_rows]
        kernel_rows.append(
            jnp.sum(
                grad_conv
                * padded_glu[kernel_len - 1 - offset : kernel_len - 1 - offset + tok_rows],
                axis=0,
            )
        )
    kernel_portion = jnp.stack(kernel_rows, axis=0)
    grad_value = grad_glu * gate_sig
    grad_gate = grad_glu * value_part * gate_sig * (1.0 - gate_sig)
    grad_hidden = jnp.concatenate([grad_value, grad_gate], axis=1).astype(jnp.bfloat16)
    normalized_gradient = lax.dot_general(
        grad_hidden, full_weight, (((1,), (1,)), ((), ())), preferred_element_type=jnp.float32
    )
    grad_kernel, layer_norm_gain_gradient, grad_ln_bias = tree_sum(
        (
            kernel_portion,
            jnp.sum(normalized_gradient * standardized_input, axis=0),
            jnp.sum(normalized_gradient, axis=0),
        ),
        ("seq", "fsdp"),
    )
    rescaled_rows = normalized_gradient * layer_norm_gain
    input_gradient = row_inverse_deviation * (
        rescaled_rows
        - jnp.mean(rescaled_rows, axis=-1, keepdims=True)
        - standardized_input * jnp.mean(rescaled_rows * standardized_input, axis=-1, keepdims=True)
    )
    row_share = lax.psum_scatter(
        lax.dot_general(
            normalized_rows,
            grad_hidden,
            (((0,), (0,)), ((), ())),
            preferred_element_type=jnp.float32,
        ),
        "fsdp",
        scatter_dimension=0,
        tiled=True,
    )
    grad_w_in = lax.psum(row_share, "seq")
    return (
        output,
        input_gradient.astype(jnp.bfloat16),
        grad_w_in,
        grad_kernel,
        grad_bn_gain,
        grad_bn_bias,
        layer_norm_gain_gradient,
        grad_ln_bias,
    )


def solution(mesh):
    placed = (
        P(("seq", "fsdp"), None),
        P(),
        P(),
        P("fsdp", None),
        P(),
        P(),
        P(),
        P(("seq", "fsdp"), None),
    )
    return jax.shard_map(
        on_device,
        mesh=mesh,
        in_specs=placed,
        out_specs=(
            P(("seq", "fsdp"), None),
            P(("seq", "fsdp"), None),
            P("fsdp", None),
            P(),
            P(),
            P(),
            P(),
            P(),
        ),
        check_vma=False,
    )
```

profile of v0, /device:TPU:0, one launch (start us, length us, event | category | flops | bytes accessed | tf_op | source)
XLA Modules:
  0.0 560.9 jit_solution(14859436354774125420)
XLA Ops:
  9.3 67.3 %all-gather.2.cloned.1.call-done = bf16[1536,3072]{1,0:T(8,128)(2,1)} async-done(((bf16[384,3072]{1,0:T(8,128)(2,1)}), bf16[1536,3072]{1,0:T(8,128)(2,1)}) %all-gather.2.cloned.1.call-update) | async-done | bytes 9437200 | tf_op jit(solution)/shard_map/all_gather | solution.py:42
  76.6 6.7 %fusion.114 = f32[384,3072]{1,0:T(8,128)S(1)} fusion(bf16[1536,3072]{1,0:T(8,128)(2,1)} %all-gather.2.cloned.1.call-done, bf16[384,1536]{1,0:T(8,128)(2,1)S(1)} %copy-done.2, f32[1536]{0:T(1024)S(1)} %copy-done.10, f32[1536]{0:T(1024)S(1)} %copy-done.9, f32[384]{0:T(512)S(1)} %add_rsqrt_fusion.1, f32[384]{0:T(512)S(1)} %broadcast_multiply_fusion.3), kind=kOutput, calls=%fused_computation.258 | convolution fusion | flops 3627417600 | bytes 15350784 | tf_op jit(solution)/shard_map/dot_general | solution.py:43
  88.9 9.4 %fusion.119 = (f32[1536]{0:T(1024)S(1)}, f32[384,1536]{1,0:T(8,128)S(1)}) fusion(f32[415,1536]{1,0:T(8,128)S(1)} %maximum_convert_fusion, f32[1536]{0:T(1024)S(1)} %get-tuple-element.76, f32[1536]{0:T(1024)S(1)} %get-tuple-element.77, f32[1536]{0:T(1024)S(1)} %get-tuple-element.47, f32[1536]{0:T(1024)S(1)} %get-tuple-element.48, ...), kind=kLoop, calls=%fused_computation.261 | loop fusion | flops 37747200 | bytes 78059520 | tf_op jit(solution)/shard_map/reduce_sum | solution.py:56
  100.2 2.6 collective-permute-start.2
  104.4 4.1 collective-permute-start.3
  110.2 2.9 collective-permute-start.4
  114.7 2.9 collective-permute-start.5
  120.8 3.6 collective-permute-done.7
  125.6 2.6 collective-permute-done.8
  131.8 2.9 collective-permute-start.10
  136.4 2.5 fusion.116
  151.0 2.9 collective-permute-start.15
  158.5 7.1 %multiply_reduce_fusion = (f32[1536]{0:T(1024)S(1)}, f32[1536]{0:T(1024)S(1)}, f32[1536]{0:T(1024)S(1)}, f32[1536]{0:T(1024)S(1)}, f32[1536]{0:T(1024)S(1)}, /*i...) fusion(f32[415,1536]{1,0:T(8,128)S(1)} %maximum_convert_fusion,, ...), kind=kLoop, calls=%fused_computation.169 | loop fusion | flops 31822848 | bytes 48519168 | tf_op jit(solution)/shard_map/reduce_sum | solution.py:78
  170.3 40.4 %multiply_convert_fusion.1 = (bf16[384,1536]{1,0:T(8,128)(2,1)S(1)}, f32[384,1536]{1,0:T(8,128)}) fusion(f32[384,3072]{1,0:T(8,128)} %copy-done, f32[31,1536]{1,0:T(8,128)S(1)} %collective-permute-done.21, f32[384,1536]{1,0:T(8,128)} %copy-done.1, f32[1536]{0:T(1024)S(1)} %get-tuple-element.76, f32[1536]{0:T(1024)S(1)} %get-tuple-element.77, ...), kind=kLoop, calls=%fused_computation.202 | loop fusion | flops 58392576 | bytes 8644608 | tf_op jit(solution)/shard_map/convert
  210.8 4.4 multiply_convert_fusion
  216.3 9.4 %fusion.109 = f32[1536,3072]{1,0:T(8,128)} fusion(bf16[384,1536]{1,0:T(8,128)(2,1)S(1)} %multiply_convert_fusion, bf16[384,1536]{1,0:T(8,128)(2,1)S(1)} %get-tuple-element.79, bf16[384,1536]{1,0:T(8,128)(2,1)S(1)} %copy-done.3, f32[1536]{0:T(1024)S(1)} %copy-done.10, f32[1536]{0:T(1024)S(1)} %copy-done.9, f32[384]{0:T(512)S(1)} %add_rsqrt_fusion.1, ...), kind=kOutput, calls=%fused_computation.214 | convolution fusion | flops 3632136192 | bytes 22428672 | tf_op jit(solution)/shard_map/dot_general | solution.py:106
  226.0 140.8 %reduce-scatter.2.cloned.1.call-done = f32[384,3072]{1,0:T(8,128)} async-done(((f32[1536,3072]{1,0:T(8,128)}), f32[384,3072]{1,0:T(8,128)}) %reduce-scatter.2.cloned.1.call-update) | async-done | bytes 4718608 | tf_op jit(solution)/shard_map/reduce_scatter | solution.py:105
  366.8 5.4 multiply_reduce_fusion.18
  374.9 6.6 %collective-permute-done.23 = f32[32,1536]{1,0:T(8,128)S(1)} collective-permute-done((f32[32,1536]{1,0:T(8,128)S(1)}, f32[32,1536]{1,0:T(8,128)S(1)}, u32[]{:S(2)}, u32[]{:S(2)}) %collective-permute-start.23) | collective-permute-done | bytes 196640 | tf_op jit(solution)/shard_map/ppermute | solution.py:22
  383.1 9.1 %fusion.12 = (f32[1536]{0:T(1024)S(1)}, f32[384]{0:T(512)S(1)}, f32[384]{0:T(512)S(1)}, f32[1536]{0:T(1024)S(1)}, f32[384,1536]{1,0:T(8,128)S(1)}) fusion(bf16[384,1536]{1,0:T(8,128)(2,1)} %param.8, f32[384]{0:T(512)S(1)} %add_rsqrt_fusion.1, f32[384]{0:T(512)S(1)} %broadcast_multiply_fusion.3, f32[1536]{0:T(1024)S(1)} %copy-done.9, ...), kind=kOutput, calls=%fused_computation.44 | convolution fusion | flops 3634491392 | bytes 15360000 | tf_op jit(solution)/shard_map/dot_general | solution.py:88
  409.5 17.2 %collective-permute-done.25 = f32[32,1536]{1,0:T(8,128)S(1)} collective-permute-done((f32[32,1536]{1,0:T(8,128)S(1)}, f32[32,1536]{1,0:T(8,128)S(1)}, u32[]{:S(2)}, u32[]{:S(2)}) %collective-permute-start.25) | collective-permute-done | bytes 196640 | tf_op jit(solution)/shard_map/ppermute | solution.py:22
  430.3 9.8 %collective-permute-done.26 = f32[32,1536]{1,0:T(8,128)S(1)} collective-permute-done((f32[32,1536]{1,0:T(8,128)S(1)}, f32[32,1536]{1,0:T(8,128)S(1)}, u32[]{:S(2)}, u32[]{:S(2)}) %collective-permute-start.26) | collective-permute-done | bytes 196640 | tf_op jit(solution)/shard_map/ppermute | solution.py:22
  440.8 108.5 %all-reduce.2.cloned.1.call-done = f32[384,3072]{1,0:T(8,128)} async-done(((f32[384,3072]{1,0:T(8,128)}), f32[384,3072]{1,0:T(8,128)}) %all-reduce.2.cloned.1.call-update) | async-done | bytes 4718608 | tf_op jit(solution)/shard_map/psum | solution.py:116
  549.3 5.1 copy.17
  (178 shorter events, 72.1 us)
Async XLA Ops:
  7.2 69.4 %all-gather.2.cloned.1.call-start = ((), (), s32[]{:S(2)}) async-start(), calls=%async_computation.1 | async-start | bytes 11796480 | tf_op jit(solution)/shard_map/all_gather | solution.py:42
  7.9 358.8 %reduce-scatter.2.cloned.1.call-start = ((), (), s32[]{:S(2)}) async-start(), calls=%async_computation.2 | async-start | bytes 23592960 | tf_op jit(solution)/shard_map/reduce_scatter | solution.py:105
  100.2 4.3 collective-permute-start.2
  104.4 5.7 %collective-permute-start.3 = (f32[1536]{0:T(1024)S(1)}, f32[1536]{0:T(1024)S(1)}, u32[]{:S(2)}, u32[]{:S(2)}) collective-permute-start(f32[1536]{0:T(1024)S(1)} %add.374), channel_id=1, source_target_pairs={{0,4},{1,5},{2,6},{3,7},{4,0},{5,1},{6,2},{7,3},{8,12},{9,13},{10,... | collective-permute-start | bytes 18440 | tf_op jit(solution)/shard_map/ppermute | solution.py:22
  110.2 4.6 collective-permute-start.4
  114.7 4.6 collective-permute-start.5
  128.1 3.7 collective-permute-start.9
  131.8 4.6 collective-permute-start.10
  140.2 4.6 collective-permute-start.17
  144.8 4.6 collective-permute-start.18
  149.4 4.6 collective-permute-start.19
  151.0 4.5 collective-permute-start.15
  153.9 4.6 collective-permute-start.20
  225.7 323.6 %all-reduce.2.cloned.1.call-start = ((), (), s32[]{:S(2)}) async-start(), calls=%async_computation.3 | async-start | bytes 9437184 | tf_op jit(solution)/shard_map/psum | solution.py:116
  374.6 7.0 %collective-permute-start.23 = (f32[32,1536]{1,0:T(8,128)S(1)}, f32[32,1536]{1,0:T(8,128)S(1)}, u32[]{:S(2)}, u32[]{:S(2)}) collective-permute-start(f32[32,1536]{1,0:T(8,128)S(1)} %add.430), channel_id=1, source_target_pairs={{0,2},{1,3},{2,0},{3,1},{4,6},{5,7},{6,4},{7,5},{8,10},{9,11},{10,... | collective-permute-start | bytes 589832 | tf_op jit(solution)/shard_map/ppermute | solution.py:22
  381.6 21.3 %collective-permute-start.24 = (f32[32,1536]{1,0:T(8,128)S(1)}, f32[32,1536]{1,0:T(8,128)S(1)}, u32[]{:S(2)}, u32[]{:S(2)}) collective-permute-start(f32[32,1536]{1,0:T(8,128)S(1)} %add.431), channel_id=1, source_target_pairs={{0,4},{1,5},{2,6},{3,7},{4,0},{5,1},{6,2},{7,3},{8,12},{9,13},{10,... | collective-permute-start | bytes 589832 | tf_op jit(solution)/shard_map/ppermute | solution.py:22
  394.0 3.7 collective-permute-start.33
  397.7 4.6 collective-permute-start.34
  400.8 5.8 %collective-permute-start.30 = (f32[1536]{0:T(1024)S(1)}, f32[1536]{0:T(1024)S(1)}, u32[]{:S(2)}, u32[]{:S(2)}) collective-permute-start(f32[1536]{0:T(1024)S(1)} %add.437), channel_id=1, source_target_pairs={{0,8},{1,9},{2,10},{3,11},{4,12},{5,13},{6,14},{7,15},{8,0},{9,1},... | collective-permute-start | bytes 18440 | tf_op jit(solution)/shard_map/ppermute | solution.py:22
  402.3 4.8 collective-permute-start.35
  402.9 23.9 %collective-permute-start.25 = (f32[32,1536]{1,0:T(8,128)S(1)}, f32[32,1536]{1,0:T(8,128)S(1)}, u32[]{:S(2)}, u32[]{:S(2)}) collective-permute-start(f32[32,1536]{1,0:T(8,128)S(1)} %add.432), channel_id=1, source_target_pairs={{0,8},{1,9},{2,10},{3,11},{4,12},{5,13},{6,14},{7,15},{8,0},{9,1},... | collective-permute-start | bytes 589832 | tf_op jit(solution)/shard_map/ppermute | solution.py:22
  406.6 22.5 %collective-permute-start.31 = (f32[1536]{0:T(1024)S(1)}, f32[1536]{0:T(1024)S(1)}, u32[]{:S(2)}, u32[]{:S(2)}) collective-permute-start(f32[1536]{0:T(1024)S(1)} %add.438), channel_id=1, source_target_pairs={{0,16},{1,17},{2,18},{3,19},{4,20},{5,21},{6,22},{7,23},{8,24},{9,... | collective-permute-start | bytes 18440 | tf_op jit(solution)/shard_map/ppermute | solution.py:22
  407.1 22.6 %collective-permute-start.36 = (f32[1536]{0:T(1024)S(1)}, f32[1536]{0:T(1024)S(1)}, u32[]{:S(2)}, u32[]{:S(2)}) collective-permute-start(f32[1536]{0:T(1024)S(1)} %add.443), channel_id=1, source_target_pairs={{0,16},{1,17},{2,18},{3,19},{4,20},{5,21},{6,22},{7,23},{8,24},{9,... | collective-permute-start | bytes 18440 | tf_op jit(solution)/shard_map/ppermute | solution.py:22
  426.8 13.4 %collective-permute-start.26 = (f32[32,1536]{1,0:T(8,128)S(1)}, f32[32,1536]{1,0:T(8,128)S(1)}, u32[]{:S(2)}, u32[]{:S(2)}) collective-permute-start(f32[32,1536]{1,0:T(8,128)S(1)} %add.433), channel_id=1, source_target_pairs={{0,16},{1,17},{2,18},{3,19},{4,20},{5,21},{6,22},{7,23},{8,24},{9,... | collective-permute-start | bytes 589832 | tf_op jit(solution)/shard_map/ppermute | solution.py:22
  (30 other events, 364.3 us)
Sparse Core Ops, SparseCore 0:
  9.6 66.9 all-gather.1
  225.8 140.8 reduce-scatter.1
  370.8 178.4 all-reduce.1
where the time goes:
time: 561 us
  waiting for transfers between devices  387 us (69%)
  other arithmetic  75.8 us (14%)
  starting transfers between devices  48.7 us (9%)
  matrix products  25.2 us (4%)
  between operations  14.3 us (3%)
  local copies, waits for them, and re-layouts  10.4 us (2%)
    reduce_scatter x1, waiting for transfers between devices, on_device(): lax.psum_scatter(lax.dot_general(normalized_rows, grad_hidden, (((0,), (0...  141 us
    psum x1, waiting for transfers between devices, on_device(): grad_w_in = lax.psum(row_share, 'seq')  109 us
    all_gather x1, waiting for transfers between devices, on_device(): full_weight = lax.all_gather(w_in, 'fsdp', axis=0, tiled=True)  67.3 us
    ppermute x35, waiting for transfers between devices, tree_sum(): tree = jax.tree.map(lambda x: x + lax.ppermute(x, axis, route), tree)  66.7 us
    another operation x2, other arithmetic  44.9 us
    ppermute x35, starting transfers between devices, tree_sum(): tree = jax.tree.map(lambda x: x + lax.ppermute(x, axis, route), tree)  44.7 us
    reduce_sum x2, other arithmetic, on_device(): jnp.sum(grad_conv * padded_glu[kernel_len - 1 - offset:kernel_len - 1 - o...  12.6 us
  transfers between devices with their start and end apart: 40, of which 30 were waited for; matrix products, arithmetic and copies ran while one was open for 4% of the time, Pallas kernels for 0%

commit v1 on v0

--- a/solution.py
+++ b/solution.py
@@ -4,6 +4,24 @@
 from jax.sharding import PartitionSpec as P
 
 epsilon = 1e-05
+
+
+def gather_around(shard, axis, dim):
+    ways, here, step = (lax.axis_size(axis), lax.axis_index(axis), shard.shape[dim])
+    shape = [n * ways if d == dim else n for d, n in enumerate(shard.shape)]
+    full = lax.dynamic_update_slice_in_dim(
+        jnp.zeros(shape, shard.dtype), shard, here * step, axis=dim
+    )
+    going_up = going_down = shard
+    for far in range(1, ways // 2 + 1):
+        going_up = lax.ppermute(going_up, axis, [(d, (d + 1) % ways) for d in range(ways)])
+        full = lax.dynamic_update_slice_in_dim(full, going_up, (here - far) % ways * step, axis=dim)
+        if 2 * far < ways:
+            going_down = lax.ppermute(going_down, axis, [(d, (d - 1) % ways) for d in range(ways)])
+            full = lax.dynamic_update_slice_in_dim(
+                full, going_down, (here + far) % ways * step, axis=dim
+            )
+    return full
 
 
 def from_behind(block, axis, distance):
@@ -39,7 +57,7 @@
     )
     standardized_input = centered_rows * row_inverse_deviation
     normalized_rows = (standardized_input * layer_norm_gain + layer_norm_bias).astype(jnp.bfloat16)
-    full_weight = lax.all_gather(w_in, "fsdp", axis=0, tiled=True)
+    full_weight = gather_around(w_in, "fsdp", 0)
     hidden = jnp.dot(normalized_rows, full_weight, preferred_element_type=jnp.float32)
     value_part = hidden[:, :features]
     gate_sig = jax.nn.sigmoid(hidden[:, features:])

time: 561 us -> 574 us (1.023)
  local copies, waits for them, and re-layouts: 10.4 us -> 19.3 us
  starting transfers between devices: 48.7 us -> 55.8 us
    all_gather x1 -> x0, waiting for transfers between devices: 67.3 us -> none  [on_device(): full_weight = lax.all_gather(w_in, 'fsdp', axis=0, tiled=True)]
    ppermute x0 -> x3, waiting for transfers between devices: none -> 66.8 us  [the longest x2 66.8 us: gather_around(): lax.ppermute(going_up, axis, [(d, (d + 1) % ways) for d in range(ways)])]
  transfers between devices with their start and end apart: 40 -> 42, of which waited for: 30 -> 29; matrix products, arithmetic and copies ran while one was open for 4% -> 5% of each run, Pallas kernels for 0% -> 0%
where the time goes in v1:
time: 574 us; the launch traced here: 573 us
  waiting for transfers between devices  384 us (67%)
  other arithmetic  77 us (13%)
  starting transfers between devices  55.8 us (10%)
  matrix products  22.6 us (4%)
  local copies, waits for them, and re-layouts  19.3 us (3%)
  between operations  14.7 us (3%)
    reduce_scatter x1, waiting for transfers between devices, on_device(): lax.psum_scatter(lax.dot_general(normalized_rows, grad_hidden, (((0,), (0...  141 us
    psum x1, waiting for transfers between devices, on_device(): grad_w_in = lax.psum(row_share, 'seq')  109 us
    ppermute x2, waiting for transfers between devices, gather_around(): lax.ppermute(going_up, axis, [(d, (d + 1) % ways) for d in range(ways)])  66.8 us
    ppermute x35, waiting for transfers between devices, tree_sum(): tree = jax.tree.map(lambda x: x + lax.ppermute(x, axis, route), tree)  65.9 us
    another operation x2, other arithmetic  44.8 us
    ppermute x35, starting transfers between devices, tree_sum(): tree = jax.tree.map(lambda x: x + lax.ppermute(x, axis, route), tree)  44.3 us
    reduce_sum x2, other arithmetic, on_device(): jnp.sum(grad_conv * padded_glu[kernel_len - 1 - offset:kernel_len - 1 - o...  12.5 us
  transfers between devices with their start and end apart: 42, of which 29 were waited for; matrix products, arithmetic and copies ran while one was open for 5% of the time, Pallas kernels for 0%

profile of v1, /device:TPU:0, one launch (start us, length us, event | category | flops | bytes accessed | tf_op | source)
XLA Modules:
  0.0 573.4 jit_solution(12138351405461055186)
XLA Ops:
  9.7 49.3 %collective-permute-done = bf16[384,3072]{1,0:T(8,128)(2,1)S(1)} collective-permute-done((bf16[384,3072]{1,0:T(8,128)(2,1)}, bf16[384,3072]{1,0:T(8,128)(2,1)S(1)}, u32[]{:S(2)}, u32[]{:S(2)}) %collective-permute-start) | collective-permute-done | bytes 2359328 | tf_op jit(solution)/shard_map/ppermute | solution.py:17
  59.0 2.6 collective-permute-start.2
  69.9 17.5 %collective-permute-done.2 = bf16[384,3072]{1,0:T(8,128)(2,1)} collective-permute-done((bf16[384,3072]{1,0:T(8,128)(2,1)S(1)}, bf16[384,3072]{1,0:T(8,128)(2,1)}, u32[]{:S(2)}, u32[]{:S(2)}) %collective-permute-start.2) | collective-permute-done | bytes 2359328 | tf_op jit(solution)/shard_map/ppermute | solution.py:17
  89.4 4.1 fusion.114
  95.7 4.5 collective-permute-start.3
  102.1 9.4 %fusion.119 = (f32[1536]{0:T(1024)S(1)}, f32[384,1536]{1,0:T(8,128)S(1)}) fusion(f32[415,1536]{1,0:T(8,128)S(1)} %maximum_convert_fusion, f32[1536]{0:T(1024)S(1)} %get-tuple-element.76, f32[1536]{0:T(1024)S(1)} %get-tuple-element.77, f32[1536]{0:T(1024)S(1)} %get-tuple-element.47, f32[1536]{0:T(1024)S(1)} %get-tuple-element.48, ...), kind=kLoop, calls=%fused_computation.265 | loop fusion | flops 37747200 | bytes 78059520 | tf_op jit(solution)/shard_map/reduce_sum | solution.py:74
  111.6 2.6 collective-permute-start.4
  115.1 2.5 collective-permute-start.5
  126.6 3.0 collective-permute-start.8
  137.4 2.7 collective-permute-done.11
  143.8 2.9 collective-permute-start.13
  163.0 2.9 collective-permute-start.18
  170.5 7.1 %multiply_reduce_fusion = (f32[1536]{0:T(1024)S(1)}, f32[1536]{0:T(1024)S(1)}, f32[1536]{0:T(1024)S(1)}, f32[1536]{0:T(1024)S(1)}, f32[1536]{0:T(1024)S(1)}, /*i...) fusion(f32[415,1536]{1,0:T(8,128)S(1)} %maximum_convert_fusion,, ...), kind=kLoop, calls=%fused_computation.169 | loop fusion | flops 31822848 | bytes 48519168 | tf_op jit(solution)/shard_map/reduce_sum | solution.py:96
  182.3 40.4 %multiply_convert_fusion.1 = (bf16[384,1536]{1,0:T(8,128)(2,1)S(1)}, f32[384,1536]{1,0:T(8,128)}) fusion(f32[384,3072]{1,0:T(8,128)} %copy-done, f32[31,1536]{1,0:T(8,128)S(1)} %collective-permute-done.24, f32[384,1536]{1,0:T(8,128)} %copy-done.1, f32[1536]{0:T(1024)S(1)} %get-tuple-element.76, f32[1536]{0:T(1024)S(1)} %get-tuple-element.77, ...), kind=kLoop, calls=%fused_computation.202 | loop fusion | flops 58392576 | bytes 8644608 | tf_op jit(solution)/shard_map/convert
  222.8 4.4 multiply_convert_fusion
  228.2 9.4 %fusion.109 = f32[1536,3072]{1,0:T(8,128)} fusion(bf16[384,1536]{1,0:T(8,128)(2,1)S(1)} %multiply_convert_fusion, bf16[384,1536]{1,0:T(8,128)(2,1)S(1)} %get-tuple-element.79, bf16[384,1536]{1,0:T(8,128)(2,1)S(1)} %copy-done.3, f32[1536]{0:T(1024)S(1)} %copy-done.11, f32[1536]{0:T(1024)S(1)} %copy-done.10, f32[384]{0:T(512)S(1)} %add_rsqrt_fusion.1, ...), kind=kOutput, calls=%fused_computation.214 | convolution fusion | flops 3632136192 | bytes 22428672 | tf_op jit(solution)/shard_map/dot_general | solution.py:124
  238.0 140.9 %reduce-scatter.2.cloned.1.call-done = f32[384,3072]{1,0:T(8,128)} async-done(((f32[1536,3072]{1,0:T(8,128)}), f32[384,3072]{1,0:T(8,128)}) %reduce-scatter.2.cloned.1.call-update) | async-done | bytes 4718608 | tf_op jit(solution)/shard_map/reduce_scatter | solution.py:123
  378.9 5.4 multiply_reduce_fusion.18
  387.1 6.6 %collective-permute-done.26 = f32[32,1536]{1,0:T(8,128)S(1)} collective-permute-done((f32[32,1536]{1,0:T(8,128)S(1)}, f32[32,1536]{1,0:T(8,128)S(1)}, u32[]{:S(2)}, u32[]{:S(2)}) %collective-permute-start.26) | collective-permute-done | bytes 196640 | tf_op jit(solution)/shard_map/ppermute | solution.py:40
  395.3 9.1 %fusion.12 = (f32[1536]{0:T(1024)S(1)}, f32[384]{0:T(512)S(1)}, f32[384]{0:T(512)S(1)}, f32[1536]{0:T(1024)S(1)}, f32[384,1536]{1,0:T(8,128)S(1)}) fusion(bf16[384,1536]{1,0:T(8,128)(2,1)} %param.8, f32[384]{0:T(512)S(1)} %add_rsqrt_fusion.1, f32[384]{0:T(512)S(1)} %broadcast_multiply_fusion.3, f32[1536]{0:T(1024)S(1)} %copy-done.10, ...), kind=kOutput, calls=%fused_computation.44 | convolution fusion | flops 3634491392 | bytes 15360000 | tf_op jit(solution)/shard_map/dot_general | solution.py:106
  421.7 17.2 %collective-permute-done.28 = f32[32,1536]{1,0:T(8,128)S(1)} collective-permute-done((f32[32,1536]{1,0:T(8,128)S(1)}, f32[32,1536]{1,0:T(8,128)S(1)}, u32[]{:S(2)}, u32[]{:S(2)}) %collective-permute-start.28) | collective-permute-done | bytes 196640 | tf_op jit(solution)/shard_map/ppermute | solution.py:40
  442.5 9.8 %collective-permute-done.29 = f32[32,1536]{1,0:T(8,128)S(1)} collective-permute-done((f32[32,1536]{1,0:T(8,128)S(1)}, f32[32,1536]{1,0:T(8,128)S(1)}, u32[]{:S(2)}, u32[]{:S(2)}) %collective-permute-start.29) | collective-permute-done | bytes 196640 | tf_op jit(solution)/shard_map/ppermute | solution.py:40
  453.0 108.5 %all-reduce.2.cloned.1.call-done = f32[384,3072]{1,0:T(8,128)} async-done(((f32[384,3072]{1,0:T(8,128)}), f32[384,3072]{1,0:T(8,128)}) %all-reduce.2.cloned.1.call-update) | async-done | bytes 4718608 | tf_op jit(solution)/shard_map/psum | solution.py:134
  561.5 5.1 copy.21
  (188 shorter events, 90.5 us)
Async XLA Ops:
  7.2 371.7 %reduce-scatter.2.cloned.1.call-start = ((), (), s32[]{:S(2)}) async-start(), calls=%async_computation.1 | async-start | bytes 23592960 | tf_op jit(solution)/shard_map/reduce_scatter | solution.py:123
  7.2 51.8 %collective-permute-start = (bf16[384,3072]{1,0:T(8,128)(2,1)}, bf16[384,3072]{1,0:T(8,128)(2,1)S(1)}, u32[]{:S(2)}, u32[]{:S(2)}) collective-permute-start(bf16[384,3072]{1,0:T(8,128)(2,1)} %param.11), channel_id=1, source_target_pairs={{0,1},{1,2},{2,3},{3,0},{4,5},{5,6},{6,7},{7,4},{8,9},{9,10},{10,1... | collective-permute-start | bytes 7077896 | tf_op jit(solution)/shard_map/ppermute | solution.py:17
  7.7 60.2 %collective-permute-start.1 = (bf16[384,3072]{1,0:T(8,128)(2,1)}, bf16[384,3072]{1,0:T(8,128)(2,1)}, u32[]{:S(2)}, u32[]{:S(2)}) collective-permute-start(bf16[384,3072]{1,0:T(8,128)(2,1)} %param.11), channel_id=1, source_target_pairs={{0,3},{1,0},{2,1},{3,2},{4,7},{5,4},{6,5},{7,6},{8,11},{9,8},{10,9... | collective-permute-start | bytes 7077896 | tf_op jit(solution)/shard_map/ppermute | solution.py:20
  59.0 28.4 %collective-permute-start.2 = (bf16[384,3072]{1,0:T(8,128)(2,1)S(1)}, bf16[384,3072]{1,0:T(8,128)(2,1)}, u32[]{:S(2)}, u32[]{:S(2)}) collective-permute-start(bf16[384,3072]{1,0:T(8,128)(2,1)S(1)} %collective-permute-done), channel_id=1, source_target_pairs={{0,1},{1,2},{2,3},{3,0},{4,5},{5,6},{6,7},{7,4},{8,9},{9,10},{10,1... | collective-permute-start | bytes 7077896 | tf_op jit(solution)/shard_map/ppermute | solution.py:17
  95.7 6.1 %collective-permute-start.3 = (bf16[31,1536]{1,0:T(8,128)(2,1)S(1)}, bf16[31,1536]{1,0:T(8,128)(2,1)S(1)}, u32[]{:S(2)}, u32[]{:S(2)}) collective-permute-start(bf16[31,1536]{1,0:T(8,128)(2,1)S(1)} %slice.462), channel_id=1, source_target_pairs={{0,1},{1,2},{2,3},{3,4},{4,5},{5,6},{6,7},{7,8},{8,9},{9,10},{10,1... | collective-permute-start | bytes 285704 | tf_op jit(solution)/shard_map/ppermute | solution.py:30
  115.1 4.1 collective-permute-start.5
  122.9 3.8 collective-permute-start.7
  126.6 4.7 collective-permute-start.8
  143.8 4.5 collective-permute-start.13
  153.8 3.7 collective-permute-start.20
  157.5 3.8 collective-permute-start.21
  161.3 4.7 collective-permute-start.22
  163.0 4.6 collective-permute-start.18
  165.9 4.6 collective-permute-start.23
  237.7 323.9 %all-reduce.2.cloned.1.call-start = ((), (), s32[]{:S(2)}) async-start(), calls=%async_computation.2 | async-start | bytes 9437184 | tf_op jit(solution)/shard_map/psum | solution.py:134
  386.7 7.0 %collective-permute-start.26 = (f32[32,1536]{1,0:T(8,128)S(1)}, f32[32,1536]{1,0:T(8,128)S(1)}, u32[]{:S(2)}, u32[]{:S(2)}) collective-permute-start(f32[32,1536]{1,0:T(8,128)S(1)} %add.465), channel_id=1, source_target_pairs={{0,2},{1,3},{2,0},{3,1},{4,6},{5,7},{6,4},{7,5},{8,10},{9,11},{10,... | collective-permute-start | bytes 589832 | tf_op jit(solution)/shard_map/ppermute | solution.py:40
  393.8 21.3 %collective-permute-start.27 = (f32[32,1536]{1,0:T(8,128)S(1)}, f32[32,1536]{1,0:T(8,128)S(1)}, u32[]{:S(2)}, u32[]{:S(2)}) collective-permute-start(f32[32,1536]{1,0:T(8,128)S(1)} %add.466), channel_id=1, source_target_pairs={{0,4},{1,5},{2,6},{3,7},{4,0},{5,1},{6,2},{7,3},{8,12},{9,13},{10,... | collective-permute-start | bytes 589832 | tf_op jit(solution)/shard_map/ppermute | solution.py:40
  409.9 4.6 collective-permute-start.37
  413.0 5.8 %collective-permute-start.33 = (f32[1536]{0:T(1024)S(1)}, f32[1536]{0:T(1024)S(1)}, u32[]{:S(2)}, u32[]{:S(2)}) collective-permute-start(f32[1536]{0:T(1024)S(1)} %add.472), channel_id=1, source_target_pairs={{0,8},{1,9},{2,10},{3,11},{4,12},{5,13},{6,14},{7,15},{8,0},{9,1},... | collective-permute-start | bytes 18440 | tf_op jit(solution)/shard_map/ppermute | solution.py:40
  414.5 4.8 collective-permute-start.38
  415.1 23.9 %collective-permute-start.28 = (f32[32,1536]{1,0:T(8,128)S(1)}, f32[32,1536]{1,0:T(8,128)S(1)}, u32[]{:S(2)}, u32[]{:S(2)}) collective-permute-start(f32[32,1536]{1,0:T(8,128)S(1)} %add.467), channel_id=1, source_target_pairs={{0,8},{1,9},{2,10},{3,11},{4,12},{5,13},{6,14},{7,15},{8,0},{9,1},... | collective-permute-start | bytes 589832 | tf_op jit(solution)/shard_map/ppermute | solution.py:40
  418.8 22.5 %collective-permute-start.34 = (f32[1536]{0:T(1024)S(1)}, f32[1536]{0:T(1024)S(1)}, u32[]{:S(2)}, u32[]{:S(2)}) collective-permute-start(f32[1536]{0:T(1024)S(1)} %add.473), channel_id=1, source_target_pairs={{0,16},{1,17},{2,18},{3,19},{4,20},{5,21},{6,22},{7,23},{8,24},{9,... | collective-permute-start | bytes 18440 | tf_op jit(solution)/shard_map/ppermute | solution.py:40
  419.3 22.6 %collective-permute-start.39 = (f32[1536]{0:T(1024)S(1)}, f32[1536]{0:T(1024)S(1)}, u32[]{:S(2)}, u32[]{:S(2)}) collective-permute-start(f32[1536]{0:T(1024)S(1)} %add.478), channel_id=1, source_target_pairs={{0,16},{1,17},{2,18},{3,19},{4,20},{5,21},{6,22},{7,23},{8,24},{9,... | collective-permute-start | bytes 18440 | tf_op jit(solution)/shard_map/ppermute | solution.py:40
  438.9 13.4 %collective-permute-start.29 = (f32[32,1536]{1,0:T(8,128)S(1)}, f32[32,1536]{1,0:T(8,128)S(1)}, u32[]{:S(2)}, u32[]{:S(2)}) collective-permute-start(f32[32,1536]{1,0:T(8,128)S(1)} %add.468), channel_id=1, source_target_pairs={{0,16},{1,17},{2,18},{3,19},{4,20},{5,21},{6,22},{7,23},{8,24},{9,... | collective-permute-start | bytes 589832 | tf_op jit(solution)/shard_map/ppermute | solution.py:40
  (33 other events, 333.7 us)
Sparse Core Ops, SparseCore 0:
  237.8 141.0 reduce-scatter.1
  382.9 178.5 all-reduce.1
